TPU v7x, 256 devices: a whole 4x4x8 slice. The times are simulated.
256 devices in a mesh: gx: 8 (over x, core), gy: 8 (over z), gz: 4 (over y).
Axes of the slice: x: 4, y: 4, z: 8, core: 2. Of those that a mesh axis runs over, the one named last changes fastest.
Arguments:
- flat_weight: float32 [6144, 128, 128], P(('gx', 'gy', 'gz')), may hold values from -6 to 6
- flat_first: float32 [6144, 128, 128], P(('gx', 'gy', 'gz')), may hold values from -3 to 3
- flat_second: float32 [6144, 128, 128], P(('gx', 'gy', 'gz')), may hold values from 0.01 to 1
- tile_map: int32 [6144], P(('gx', 'gy', 'gz')), may hold values from 0 to 6143, as said below
- tile_seeds: int32 [64, 96], P(('gx', 'gy'), 'gz'), may hold values from 0 to 16777215
- tokens: bfloat16 [3072, 12288], P(('gy', 'gx'), 'gz'), may hold values from -6 to 6
- grad_out: bfloat16 [3072, 8192], P('gy', ('gx', 'gz')), may hold values from -6 to 6
Outputs:
- outputs: bfloat16 [3072, 8192], P('gy', ('gx', 'gz'))
- input_grad: bfloat16 [3072, 12288], P(('gy', 'gx'), 'gz')
- weight_new: float32 [8192, 12288], P(('gx', 'gy'), 'gz')
- first_new: float32 [8192, 12288], P(('gx', 'gy'), 'gz')
- second_new: float32 [8192, 12288], P(('gx', 'gy'), 'gz')
Inputs may be any that keep to these rules, and one draw needn't show every extreme that they name: `tile_map`: every tile of the slab is held by exactly one slot. Device rank r = ((a * 8) + b) * 4 + c holds slots r * 24 onward; it holds only tiles of the block owned by some device with the same b, where the owner of rows 128 * R onward and columns 128 * C onward has a = R // 8, b = (R) % 8, c = C // 24. One device holds at most 2 tiles of one owner, and exactly 2 of some owner.
All inputs are finite; a program needn't handle non-finite values.
Results may differ from a plain program's by a relative error of at most 0.013.
Values may be sent and summed in bfloat16 or wider, within the bound.
No kernel may reach another device: no remote copies, remote signals or barrier semaphores. Data moves between devices by JAX's collectives and lax.ppermute only.
A program may use at most 128 MiB of HBM per device.

v0:
```python
import math
import jax
import jax.numpy as jnp
from jax import lax
from jax.sharding import PartitionSpec as P

D = 12288
BETA_ONE = 0.9
BETA_TWO = 0.95
LEARN_RATE = 0.01
WEIGHT_DECAY = 0.1
EPSILON = 1e-08
BIAS_ONE = 0.9999734386011125
BIAS_TWO = 0.994079470779666
DITHER_SCALE = 0.25


def dither(seeds, position):
    mixing = seeds + position * 1640531527
    mixing = mixing ^ mixing >> 15 & 131071
    mixing = mixing * 739982445
    mixing = mixing ^ mixing >> 12 & 1048575
    mixing = mixing * 695872825
    mixing = mixing ^ mixing >> 15 & 131071
    return (mixing & 65535).astype(jnp.float32) / 65536.0 - 0.5


def body(flat_weight, flat_first, flat_second, tile_map, tile_seeds, tokens, grad_out):
    size_gx = lax.axis_size("gx")
    size_gy = lax.axis_size("gy")
    size_gz = lax.axis_size("gz")
    group_size = size_gx * size_gz
    tiles_own = flat_weight.shape[0]
    tile_side = flat_weight.shape[1]
    row_tiles = tile_seeds.shape[0]
    col_tiles = tile_seeds.shape[1]
    capacity = max(2, (2 * tiles_own + group_size - 1) // group_size - 1)
    total_slots = group_size * capacity
    across = col_tiles * size_gz
    row_block = tile_map // across
    col_block = tile_map % across
    target = row_block // row_tiles // size_gy * size_gz + col_block // col_tiles
    local_tile = row_block % row_tiles * col_tiles + col_block % col_tiles
    ordinal = jnp.arange(tiles_own, dtype=jnp.int32)
    same_owner = (target[:, None] == target[None, :]) & (ordinal[None, :] < ordinal[:, None])
    ranking = jnp.sum(same_owner.astype(jnp.int32), axis=1)
    position = target * capacity + ranking
    slot_ids = jnp.arange(total_slots, dtype=jnp.int32)
    matches = (position[None, :] == slot_ids[:, None]).astype(jnp.int32)
    source = jnp.sum(matches * ordinal[None, :], axis=1)
    filled = jnp.sum(matches, axis=1).astype(jnp.float32)[:, None, None]
    labels = jnp.sum(matches * (local_tile[None, :] + 1), axis=1)
    grid_shape = (group_size, capacity, tile_side, tile_side)
    send_weight = (jnp.take(flat_weight, source, axis=0) * filled).astype(jnp.bfloat16)
    got_labels = lax.all_to_all(
        labels.reshape(group_size, capacity), ("gx", "gz"), split_axis=0, concat_axis=0, tiled=True
    )
    got_weight = lax.all_to_all(
        send_weight.reshape(grid_shape), ("gx", "gz"), split_axis=0, concat_axis=0, tiled=True
    )
    token_band = lax.all_gather(tokens, "gx", axis=0, tiled=True)
    got_weight, token_band = lax.optimization_barrier((got_weight, token_band))
    got_weight = got_weight.astype(jnp.float32)
    got_labels = got_labels.reshape(total_slots)
    wanted = jnp.arange(1, tiles_own + 1, dtype=jnp.int32)
    hits = (got_labels[None, :] == wanted[:, None]).astype(jnp.int32)
    picked = jnp.sum(hits * slot_ids[None, :], axis=1)

    def place(received):
        flat_tiles = jnp.take(received.reshape(total_slots, tile_side, tile_side), picked, axis=0)
        tile_grid = flat_tiles.reshape(row_tiles, col_tiles, tile_side, tile_side)
        return tile_grid.transpose(0, 2, 1, 3).reshape(row_tiles * tile_side, col_tiles * tile_side)

    weight = place(got_weight)
    weight_low = weight.astype(jnp.bfloat16)
    weight_band = lax.all_gather(weight_low, "gy", axis=0, tiled=True)
    send_moments = jnp.stack(
        [
            jnp.take(flat_first, source, axis=0) * filled,
            jnp.take(flat_second, source, axis=0) * filled,
        ],
        axis=1,
    ).astype(jnp.bfloat16)
    send_moments, weight_band = lax.optimization_barrier((send_moments, weight_band))
    got_moments = (
        lax.all_to_all(
            send_moments.reshape(group_size, capacity, 2, tile_side, tile_side),
            ("gx", "gz"),
            split_axis=0,
            concat_axis=0,
            tiled=True,
        )
        .astype(jnp.float32)
        .reshape(total_slots, 2, tile_side, tile_side)
    )
    first_moment = place(got_moments[:, 0])
    second_moment = place(got_moments[:, 1])
    factor = 1.0 / math.sqrt(D)
    partial_out = factor * jnp.dot(token_band, weight_band.T, preferred_element_type=jnp.float32)
    outputs = lax.psum_scatter(
        partial_out.astype(jnp.bfloat16), "gz", scatter_dimension=1, tiled=True
    )
    grad_band = lax.all_gather(grad_out.T, "gz", axis=0, tiled=True).T
    input_grad = lax.psum_scatter(
        (factor * jnp.dot(grad_band, weight_band, preferred_element_type=jnp.float32)).astype(
            jnp.bfloat16
        ),
        "gx",
        scatter_dimension=0,
        tiled=True,
    )
    gradient = lax.psum_scatter(
        (
            factor
            * lax.dot_general(
                grad_band, token_band, (((0,), (0,)), ((), ())), preferred_element_type=jnp.float32
            )
        ).astype(jnp.bfloat16),
        "gy",
        scatter_dimension=0,
        tiled=True,
    ).astype(jnp.float32)
    first_new = BETA_ONE * first_moment + (1.0 - BETA_ONE) * gradient
    second_new = BETA_TWO * second_moment + (1.0 - BETA_TWO) * gradient * gradient
    direction = (
        first_new / BIAS_ONE / (jnp.sqrt(second_new / BIAS_TWO) + EPSILON) + WEIGHT_DECAY * weight
    )
    moved = weight - LEARN_RATE * direction
    block_shape = weight.shape
    row_ids = lax.broadcasted_iota(jnp.int32, block_shape, 0)
    col_ids = lax.broadcasted_iota(jnp.int32, block_shape, 1)
    seed_full = jnp.repeat(jnp.repeat(tile_seeds, tile_side, axis=0), tile_side, axis=1)
    noise = dither(seed_full, row_ids % tile_side * tile_side + col_ids % tile_side)
    weight_new = moved + jnp.abs(moved) * DITHER_SCALE * noise
    return (outputs, input_grad, weight_new, first_new, second_new)


def solution(mesh):
    return jax.shard_map(
        body,
        mesh=mesh,
        in_specs=(
            P(("gx", "gy", "gz"), None, None),
            P(("gx", "gy", "gz"), None, None),
            P(("gx", "gy", "gz"), None, None),
            P(("gx", "gy", "gz")),
            P(("gx", "gy"), "gz"),
            P(("gy", "gx"), "gz"),
            P("gy", ("gx", "gz")),
        ),
        out_specs=(
            P("gy", ("gx", "gz")),
            P(("gy", "gx"), "gz"),
            P(("gx", "gy"), "gz"),
            P(("gx", "gy"), "gz"),
            P(("gx", "gy"), "gz"),
        ),
        check_vma=False,
    )
```

profile of v0, /device:TPU:8, one launch (start us, length us, event | category | flops | bytes accessed | tf_op | source)
XLA Modules:
  0.0 306.8 jit_solution(18281767544763607784)
XLA Ops:
  7.2 0.0 copy-start
  7.2 0.0 all-gather.3.cloned.1.call-start
  7.2 0.7 all-gather.3.cloned.1.call-update
  7.9 0.7 fusion.19
  8.6 0.2 convert_reduce_fusion.1
  8.8 0.1 select_reduce_fusion.1
  8.9 0.7 all_to_all.13
  9.6 7.5 %all-to-all-start.1 = ((s32[32,1,2]{2,1,0:T(1,128)}), s32[32,1,2]{2,1,0:T(1,128)S(1)}, u32[]{:S(2)}, u32[]{:S(2)}) async-start(s32[32,1,2]{2,1,0:T(1,128)} %bitcast.4), calls=%async_computation.1 | async-start | bytes 32768 | tf_op jit(solution)/shard_map/all_to_all | solution.py:55
  17.2 0.0 copy-done
  17.2 0.0 copy-start.2
  17.2 2.8 gather_fusion.1
  20.0 0.0 copy-done.2
  20.0 2.8 gather_fusion.2
  22.8 0.0 copy-done.3
  22.8 2.8 gather_fusion
  25.6 7.6 %fusion.5 = (bf16[64,1,128,128]{3,2,1,0:T(8,128)(2,1)}, bf16[64,1,128,128]{3,2,1,0:T(8,128)(2,1)}, bf16[64,128,128]{2,1,0:T(8,128)(2,1)}) fusion(f32[64,128,128]{2,1,0:T(8,128)} %gather_fusion.1, f32[64]{0:T(128)S(1)} %convert_element_type.46, pred[64]{0:T(512)(128)(4,1)S(1)} %compare_and_fusion.1, f32[64,128,128]{2,1,0:T(8,128)} %gather_fusion.2, ...), kind=kLoop, calls=%fused_computation.20 | loop fusion | flops 9437184 | bytes 18874688 | tf_op jit(solution)/shard_map/stack | solution.py:77
  33.2 0.0 all-to-all-done.1
  33.2 7.6 %all-to-all-start = ((bf16[32,2,128,128]{3,2,1,0:T(8,128)(2,1)}), bf16[32,2,128,128]{3,2,1,0:T(8,128)(2,1)}, u32[]{:S(2)}, u32[]{:S(2)}) async-start(bf16[32,2,128,128]{3,2,1,0:T(8,128)(2,1)} %bitcast.65), calls=%async_computation | async-start | bytes 4194304 | tf_op jit(solution)/shard_map/all_to_all | solution.py:58
  40.8 0.0 all-gather.5.cloned.1.call-start
  40.9 0.5 broadcast.207
  41.4 0.7 reduce.3
  42.1 0.1 eq.54
  42.2 0.2 select_reduce_fusion
  42.4 25.4 %all-to-all-done = bf16[32,2,128,128]{3,2,1,0:T(8,128)(2,1)} async-done(((bf16[32,2,128,128]{3,2,1,0:T(8,128)(2,1)}), bf16[32,2,128,128]{3,2,1,0:T(8,128)(2,1)}, u32[]{:S(2)}, u32[]{:S(2)}) %all-to-all-start) | async-done | bytes 2097184 | tf_op jit(solution)/shard_map/all_to_all | solution.py:58
  67.8 4.1 %bitcast_convert_fusion = f32[64,128,128]{2,1,0:T(8,128)} fusion(bf16[32,2,128,128]{3,2,1,0:T(8,128)(2,1)} %all-to-all-done), kind=kLoop, calls=%fused_computation.22 | loop fusion | flops 1048576 | bytes 6291456 | tf_op jit(solution)/shard_map/reshape | solution.py:70
  71.9 2.8 gather_fusion.3
  74.7 0.2 select_bitcast_fusion
  74.9 0.5 copy.42
  75.4 0.0 copy-start.5
  75.4 1.0 bitcast_convert_fusion.1
  76.3 0.0 all-gather.5.cloned.1.call-update
  76.4 0.0 reduce-scatter.12.cloned.1.call-start
  76.4 14.6 %all_gather.11 = bf16[1024,384]{0,1:T(8,128)(2,1)S(1)} all-gather(bf16[256,384]{0,1:T(8,128)(2,1)S(1)} %bitcast.66), channel_id=1, replica_groups=mesh['gx'=8,'gy'=8,'gz'=4] {'gz'}, dimensions={0}, use_global_device_ids=true | all-gather | bytes 983040 | tf_op jit(solution)/shard_map/all_gather | solution.py:103
  91.1 7.2 %fusion = bf16[1024,3072]{0,1:T(8,128)(2,1)} fusion(bf16[384,3072]{1,0:T(8,128)(2,1)} %all-gather.3.cloned.1.call-done, bf16[1024,384]{0,1:T(8,128)(2,1)S(1)} %all_gather.11), kind=kOutput, calls=%fused_computation.7 | convolution fusion | flops 2422210560 | bytes 9437184 | tf_op jit(solution)/shard_map/dot_general | solution.py:115
  98.2 8.6 %copy.53 = bf16[1024,3072]{1,0:T(8,128)(2,1)} copy(bf16[1024,3072]{0,1:T(8,128)(2,1)} %fusion) | data formatting | bytes 12582912
  106.9 0.0 reduce-scatter.12.cloned.1.call-update
  106.9 0.0 reduce-scatter.8.cloned.1.call-start
  107.0 4.6 %pad_maximum_fusion = bf16[64,2,128,128]{3,2,1,0:T(8,128)(2,1)} fusion(bf16[64,1,128,128]{3,2,1,0:T(8,128)(2,1)} %get-tuple-element.49, bf16[64,1,128,128]{3,2,1,0:T(8,128)(2,1)} %get-tuple-element.48), kind=kLoop, calls=%fused_computation.11 | loop fusion | flops 2097152 | bytes 8388608 | tf_op jit(solution)/shard_map/stack | solution.py:77
  111.5 46.1 %all-gather.5.cloned.1.call-done = bf16[1024,3072]{0,1:T(8,128)(2,1)} async-done(((bf16[128,3072]{0,1:T(8,128)(2,1)}), bf16[1024,3072]{0,1:T(8,128)(2,1)}) %all-gather.5.cloned.1.call-update) | async-done | bytes 6291472 | tf_op jit(solution)/shard_map/all_gather | solution.py:76
  157.7 7.0 %multiply_convert_fusion.2 = bf16[384,1024]{1,0:T(8,128)(2,1)} fusion(bf16[384,3072]{1,0:T(8,128)(2,1)} %all-gather.3.cloned.1.call-done, bf16[1024,3072]{0,1:T(8,128)(2,1)} %all-gather.5.cloned.1.call-done), kind=kOutput, calls=%fused_computation.37 | convolution fusion | flops 2416705536 | bytes 9437184 | tf_op jit(solution)/shard_map/dot_general | solution.py:99
  164.7 0.0 reduce-scatter.8.cloned.1.call-update
  164.7 4.7 %copy.43 = bf16[32,2,2,128,128]{4,3,1,2,0:T(8,128)(2,1)} copy(bf16[32,2,2,128,128]{4,3,2,1,0:T(8,128)(2,1)} %bitcast.64) | data formatting | bytes 8388608 | tf_op jit(solution)/shard_map/reshape | solution.py:87
  169.4 7.5 %all-to-all-start.2 = ((bf16[32,2,2,128,128]{4,3,1,2,0:T(8,128)(2,1)}), bf16[32,2,2,128,128]{4,3,1,2,0:T(8,128)(2,1)}, u32[]{:S(2)}, u32[]{:S(2)}) async-start(bf16[32,2,2,128,128]{4,3,1,2,0:T(8,128)(2,1)} %copy.43), calls=%async_computation.3 | async-start | bytes 8388608 | tf_op jit(solution)/shard_map/all_to_all | solution.py:86
  176.8 0.2 reduce-scatter.10.cloned.1.call-start
  177.1 7.7 %fusion.4 = bf16[384,3072]{0,1:T(8,128)(2,1)} fusion(bf16[1024,3072]{0,1:T(8,128)(2,1)} %all-gather.5.cloned.1.call-done, bf16[1024,384]{0,1:T(8,128)(2,1)S(1)} %all_gather.11), kind=kOutput, calls=%fused_computation.18 | convolution fusion | flops 2418278400 | bytes 9437184 | tf_op jit(solution)/shard_map/dot_general | solution.py:105
  184.8 4.3 %copy.51 = bf16[384,3072]{1,0:T(8,128)(2,1)} copy(bf16[384,3072]{0,1:T(8,128)(2,1)} %fusion.4) | data formatting | bytes 4718592
  189.1 0.0 reduce-scatter.10.cloned.1.call-update
  189.2 0.6 copy-done.6
  189.8 0.1 broadcast_bitcast_fusion
  189.8 43.8 %reduce-scatter.12.cloned.1.call-done = bf16[128,3072]{1,0:T(8,128)(2,1)} async-done(((bf16[1024,3072]{1,0:T(8,128)(2,1)}), bf16[128,3072]{1,0:T(8,128)(2,1)}) %reduce-scatter.12.cloned.1.call-update) | async-done | bytes 786448
  233.6 2.3 copy.54
  235.9 0.0 all-to-all-done.2
  235.9 3.2 %copy.44 = f32[32,2,2,128,128]{4,3,1,0,2:T(8,128)S(1)} copy(bf16[32,2,2,128,128]{4,3,1,2,0:T(8,128)(2,1)} %all-to-all-done.2) | data formatting | bytes 12582912 | tf_op jit(solution)/shard_map/reshape | solution.py:94
  239.2 3.8 %slice_bitcast_fusion = (f32[64,128,128]{2,1,0:T(8,128)}, f32[64,128,128]{2,1,0:T(8,128)}) fusion(f32[64,2,128,128]{3,2,0,1:T(8,128)S(1)} %bitcast.63), kind=kLoop, calls=%fused_computation.9 | loop fusion | bytes 16777216 | tf_op jit(solution)/shard_map/squeeze | solution.py:97
  243.0 4.0 %gather_fusion.5 = f32[24,128,128]{2,1,0:T(8,128)} fusion(f32[64,128,128]{2,1,0:T(8,128)} %get-tuple-element.46, s32[1024]{0:T(1024)S(1)} %pad_clamp_fusion), kind=kCustom, calls=%fused_computation.5.clone | custom fusion | bytes 3145824 | tf_op jit(solution)/shard_map/jit(_take)/gather | solution.py:70
  247.0 4.0 %gather_fusion.4 = f32[24,128,128]{2,1,0:T(8,128)} fusion(f32[64,128,128]{2,1,0:T(8,128)} %get-tuple-element.47, s32[1024]{0:T(1024)S(1)} %pad_clamp_fusion), kind=kCustom, calls=%fused_computation.4.clone | custom fusion | bytes 3145824 | tf_op jit(solution)/shard_map/jit(_take)/gather | solution.py:70
  250.9 3.6 %fusion.11 = (f32[1,128,24,128]{3,1,2,0:T(8,128)S(1)}, f32[1,128,24,128]{3,1,2,0:T(8,128)}) fusion(f32[24,128,128]{2,1,0:T(8,128)} %gather_fusion.5, pred[24]{0:T(512)(128)(4,1)S(1)} %compare_and_fusion, f32[24,128,128]{2,1,0:T(8,128)} %gather_fusion.4), kind=kLoop, calls=%fused_computation.32 | loop fusion | flops 1572864 | bytes 6291480 | tf_op jit(solution)/shard_map/mul | solution.py:124
  254.6 3.0 copy.45
  257.6 1.6 copy.46
  259.2 9.5 %multiply_add_fusion = (f32[128,3072]{0,1:T(8,128)}, f32[128,3072]{0,1:T(8,128)}, f32[128,3072]{0,1:T(8,128)S(1)}) fusion(f32[1,128,24,128]{1,3,2,0:T(8,128)S(1)} %copy.42, s32[3072]{0:T(1024)S(1)} %get-tuple-element.55, s32[3072]{0:T(1024)S(1)} %get-tuple-element.56, s32[128]{0:T(128)S(1)} %get-tuple-element.57, s32[128]{0:T(128)S(1)} %get-tuple-element.58, ...), kind=kLoop, calls=%fused_computation.36 | loop fusion | flops 15335424 | bytes 10264704 | tf_op jit(solution)/shard_map/add | solution.py:134
  268.7 3.1 %copy.48 = f32[128,3072]{1,0:T(8,128)} copy(f32[128,3072]{0,1:T(8,128)} %get-tuple-element.43) | data formatting | bytes 3145728
  271.9 1.6 copy.49
  273.5 1.6 copy.50
  275.1 25.1 %reduce-scatter.10.cloned.1.call-done = bf16[48,3072]{1,0:T(8,128)(2,1)} async-done(((bf16[384,3072]{1,0:T(8,128)(2,1)}), bf16[48,3072]{1,0:T(8,128)(2,1)}) %reduce-scatter.10.cloned.1.call-update) | async-done | bytes 294928
  (22 shorter events, 0.1 us)
Async XLA Ops:
  7.2 10.0 %copy-start = (f32[24,128,128]{2,1,0:T(8,128)S(1)}, f32[24,128,128]{2,1,0:T(8,128)}, u32[]{:S(2)}) copy-start(f32[24,128,128]{2,1,0:T(8,128)} %param.12) | copy-start | bytes 4718596
  7.2 60.6 %all-gather.3.cloned.1.call-start = ((), (), s32[]{:S(2)}) async-start(), calls=%async_computation.6 | async-start | bytes 2654208 | tf_op jit(solution)/shard_map/all_gather | solution.py:61
  9.6 23.6 %all-to-all-start.1 = ((s32[32,1,2]{2,1,0:T(1,128)}), s32[32,1,2]{2,1,0:T(1,128)S(1)}, u32[]{:S(2)}, u32[]{:S(2)}) async-start(s32[32,1,2]{2,1,0:T(1,128)} %bitcast.4), calls=%async_computation.1 | async-start | bytes 32768 | tf_op jit(solution)/shard_map/all_to_all | solution.py:55
  17.2 2.8 copy-start.2
  20.0 2.8 copy-start.3
  33.2 34.6 %all-to-all-start = ((bf16[32,2,128,128]{3,2,1,0:T(8,128)(2,1)}), bf16[32,2,128,128]{3,2,1,0:T(8,128)(2,1)}, u32[]{:S(2)}, u32[]{:S(2)}) async-start(bf16[32,2,128,128]{3,2,1,0:T(8,128)(2,1)} %bitcast.65), calls=%async_computation | async-start | bytes 4194304 | tf_op jit(solution)/shard_map/all_to_all | solution.py:58
  40.8 116.8 %all-gather.5.cloned.1.call-start = ((), (), s32[]{:S(2)}) async-start(), calls=%async_computation.7 | async-start | bytes 7077888 | tf_op jit(solution)/shard_map/all_gather | solution.py:76
  75.4 1.0 copy-start.5
  76.4 157.3 %reduce-scatter.12.cloned.1.call-start = ((), (), s32[]{:S(2)}) async-start(), calls=%async_computation.10 | async-start | bytes 7077888
  106.9 168.2 %reduce-scatter.8.cloned.1.call-start = ((), (), s32[]{:S(2)}) async-start(), calls=%async_computation.8 | async-start | bytes 983040 | tf_op jit(solution)/shard_map/reduce_scatter | solution.py:100
  169.4 66.5 %all-to-all-start.2 = ((bf16[32,2,2,128,128]{4,3,1,2,0:T(8,128)(2,1)}), bf16[32,2,2,128,128]{4,3,1,2,0:T(8,128)(2,1)}, u32[]{:S(2)}, u32[]{:S(2)}) async-start(bf16[32,2,2,128,128]{4,3,1,2,0:T(8,128)(2,1)} %copy.43), calls=%async_computation.3 | async-start | bytes 8388608 | tf_op jit(solution)/shard_map/all_to_all | solution.py:86
  176.8 123.4 %reduce-scatter.10.cloned.1.call-start = ((), (), s32[]{:S(2)}) async-start(), calls=%async_computation.9 | async-start | bytes 2654208
  189.1 0.7 copy-start.6
  268.7 3.1 %copy-start.4 = (f32[128,3072]{0,1:T(8,128)S(1)}, f32[128,3072]{0,1:T(8,128)}, u32[]{:S(2)}) copy-start(f32[128,3072]{0,1:T(8,128)} %get-tuple-element.44) | copy-start | bytes 4718596
  273.5 26.8 %copy-start.1 = (f32[24,128,128]{2,1,0:T(8,128)S(1)}, f32[24,128,128]{2,1,0:T(8,128)}, u32[]{:S(2)}) copy-start(f32[24,128,128]{2,1,0:T(8,128)} %param.12) | copy-start | bytes 4718596
Sparse Core Ops, SparseCore 0:
  9.8 30.9 all-gather.2
  76.5 81.1 all-gather.4
  160.2 73.3 reduce-scatter.11
  236.6 21.5 reduce-scatter.7
  261.2 39.0 reduce-scatter.9
where the time goes:
time: 308 us; the launch traced here: 307 us
  waiting for transfers between devices  141 us (46%)
  local copies, waits for them, and re-layouts  59.6 us (19%)
  other arithmetic  32.4 us (11%)
  starting transfers between devices  23 us (7%)
  matrix products  21.9 us (7%)
  blocking collectives  14.6 us (5%)
  between operations  14 us (5%)
    unnamed x7, waiting for transfers between devices  69.7 us
    all_gather x1, waiting for transfers between devices, body(): weight_band = lax.all_gather(weight_low, 'gy', axis=0, tiled=True)  46.1 us
    all_to_all x1, waiting for transfers between devices, body(): lax.all_to_all(send_weight.reshape(grid_shape), ('gx', 'gz'), split_axis=...  25.4 us
    unnamed x20, local copies, waits for them, and re-layouts  22.2 us
    all_gather x1, blocking collectives, body(): grad_band = lax.all_gather(grad_out.T, 'gz', axis=0, tiled=True).T  14.6 us
    another operation x2, other arithmetic, body(): jnp.stack([jnp.take(flat_first, source, axis=0) * filled, jnp.take(flat_s...  12.2 us
    gather x3, local copies, waits for them, and re-layouts, place(): jnp.take(received.reshape(total_slots, tile_side, tile_side), picked, axi...  10.8 us
    add x1, other arithmetic, body(): weight_new = moved + jnp.abs(moved) * DITHER_SCALE * noise  9.5 us
  transfers between devices with their start and end apart: 8, of which 4 were waited for; matrix products, arithmetic and copies ran while one was open for 34% of the time, Pallas kernels for 0%

commit v1 on v0

--- a/solution.py
+++ b/solution.py
@@ -1,3 +1,4 @@
+import functools
 import math
 import jax
 import jax.numpy as jnp
@@ -13,6 +14,16 @@
 BIAS_ONE = 0.9999734386011125
 BIAS_TWO = 0.994079470779666
 DITHER_SCALE = 0.25
+
+
+def place_words_now(local, join_dim):
+    prior = jax.lax.axis_size("gz")
+    known = jnp.stack(prior * [local], axis=0)
+    value_now = jax.lax.all_to_all(known, "gz", 0, 0)
+    return jnp.concatenate(value_now, axis=join_dim)
+
+
+put_panels = functools.partial(place_words_now, join_dim=0)
 
 
 def dither(seeds, position):
@@ -100,7 +111,7 @@
     outputs = lax.psum_scatter(
         partial_out.astype(jnp.bfloat16), "gz", scatter_dimension=1, tiled=True
     )
-    grad_band = lax.all_gather(grad_out.T, "gz", axis=0, tiled=True).T
+    grad_band = put_panels(grad_out.T).T
     input_grad = lax.psum_scatter(
         (factor * jnp.dot(grad_band, weight_band, preferred_element_type=jnp.float32)).astype(
             jnp.bfloat16

time: 308 us -> 308 us (level)
    all_to_all x0 -> x1, blocking collectives: none -> 15.4 us  [place_words_now(): value_now = jax.lax.all_to_all(known, 'gz', 0, 0)]
    all_gather x1 -> x0, blocking collectives: 14.6 us -> none  [body(): grad_band = lax.all_gather(grad_out.T, 'gz', axis=0, tiled=True).T]
    unnamed x20 -> x22, local copies, waits for them, and re-layouts: 22.2 us -> 22.2 us
  transfers between devices with their start and end apart: 8 -> 8, of which waited for: 4 -> 4; matrix products, arithmetic and copies ran while one was open for 34% -> 33% of each run, Pallas kernels for 0% -> 0%
where the time goes in v1:
time: 308 us; the launch traced here: 307 us
  waiting for transfers between devices  142 us (46%)
  local copies, waits for them, and re-layouts  59.9 us (19%)
  other arithmetic  32.4 us (11%)
  starting transfers between devices  23 us (7%)
  matrix products  20.2 us (7%)
  blocking collectives  15.4 us (5%)
  between operations  14 us (5%)
    unnamed x7, waiting for transfers between devices  69.7 us
    all_gather x1, waiting for transfers between devices, body(): weight_band = lax.all_gather(weight_low, 'gy', axis=0, tiled=True)  46.8 us
    all_to_all x1, waiting for transfers between devices, body(): lax.all_to_all(send_weight.reshape(grid_shape), ('gx', 'gz'), split_axis=...  25.4 us
    unnamed x22, local copies, waits for them, and re-layouts  22.2 us
    all_to_all x1, blocking collectives, place_words_now(): value_now = jax.lax.all_to_all(known, 'gz', 0, 0)  15.4 us
    another operation x2, other arithmetic, body(): jnp.stack([jnp.take(flat_first, source, axis=0) * filled, jnp.take(flat_s...  12.2 us
    gather x3, local copies, waits for them, and re-layouts, place(): jnp.take(received.reshape(total_slots, tile_side, tile_side), picked, axi...  10.8 us
    add x1, other arithmetic, body(): weight_new = moved + jnp.abs(moved) * DITHER_SCALE * noise  9.5 us
  transfers between devices with their start and end apart: 8, of which 4 were waited for; matrix products, arithmetic and copies ran while one was open for 33% of the time, Pallas kernels for 0%

profile of v1, /device:TPU:8, one launch (start us, length us, event | category | flops | bytes accessed | tf_op | source)
XLA Modules:
  0.0 306.7 jit_solution(17567527642429593352)
XLA Ops:
  7.2 0.0 copy-start
  7.2 0.0 all-gather.3.cloned.1.call-start
  7.2 0.7 all-gather.3.cloned.1.call-update
  7.9 0.7 fusion.19
  8.6 0.2 convert_reduce_fusion.1
  8.8 0.1 select_reduce_fusion.1
  8.9 0.7 all_to_all.16
  9.6 7.5 %all-to-all-start.1 = ((s32[32,1,2]{2,1,0:T(1,128)}), s32[32,1,2]{2,1,0:T(1,128)S(1)}, u32[]{:S(2)}, u32[]{:S(2)}) async-start(s32[32,1,2]{2,1,0:T(1,128)} %bitcast.4), calls=%async_computation.1 | async-start | bytes 32768 | tf_op jit(solution)/shard_map/all_to_all | solution.py:66
  17.2 0.0 copy-start.2
  17.2 2.8 gather_fusion.1
  20.0 0.0 copy-done.2
  20.0 2.8 gather_fusion.2
  22.8 2.8 gather_fusion
  25.5 7.6 %fusion.5 = (bf16[64,1,128,128]{3,2,1,0:T(8,128)(2,1)}, bf16[64,1,128,128]{3,2,1,0:T(8,128)(2,1)}, bf16[64,128,128]{2,1,0:T(8,128)(2,1)}) fusion(f32[64,128,128]{2,1,0:T(8,128)} %gather_fusion.1, f32[64]{0:T(128)S(1)} %convert_element_type.46, pred[64]{0:T(512)(128)(4,1)S(1)} %compare_and_fusion.1, f32[64,128,128]{2,1,0:T(8,128)} %gather_fusion.2, ...), kind=kLoop, calls=%fused_computation.20 | loop fusion | flops 9437184 | bytes 18874688 | tf_op jit(solution)/shard_map/stack | solution.py:88
  33.2 0.0 all-to-all-done.1
  33.2 7.6 %all-to-all-start = ((bf16[32,2,128,128]{3,2,1,0:T(8,128)(2,1)}), bf16[32,2,128,128]{3,2,1,0:T(8,128)(2,1)}, u32[]{:S(2)}, u32[]{:S(2)}) async-start(bf16[32,2,128,128]{3,2,1,0:T(8,128)(2,1)} %bitcast.66), calls=%async_computation | async-start | bytes 4194304 | tf_op jit(solution)/shard_map/all_to_all | solution.py:69
  40.8 0.0 all-gather.5.cloned.1.call-start
  40.9 0.5 broadcast.209
  41.4 0.7 reduce.3
  42.1 0.1 eq.54
  42.2 0.2 select_reduce_fusion
  42.4 25.4 %all-to-all-done = bf16[32,2,128,128]{3,2,1,0:T(8,128)(2,1)} async-done(((bf16[32,2,128,128]{3,2,1,0:T(8,128)(2,1)}), bf16[32,2,128,128]{3,2,1,0:T(8,128)(2,1)}, u32[]{:S(2)}, u32[]{:S(2)}) %all-to-all-start) | async-done | bytes 2097184 | tf_op jit(solution)/shard_map/all_to_all | solution.py:69
  67.8 4.1 %bitcast_convert_fusion = f32[64,128,128]{2,1,0:T(8,128)} fusion(bf16[32,2,128,128]{3,2,1,0:T(8,128)(2,1)} %all-to-all-done), kind=kLoop, calls=%fused_computation.22 | loop fusion | flops 1048576 | bytes 6291456 | tf_op jit(solution)/shard_map/reshape | solution.py:81
  71.9 2.8 gather_fusion.3
  74.7 0.2 select_bitcast_fusion
  74.9 0.5 copy.46
  75.4 0.0 copy-start.5
  75.4 1.0 bitcast_convert_fusion.1
  76.3 0.0 all-gather.5.cloned.1.call-update
  76.4 0.0 reduce-scatter.12.cloned.1.call-start
  76.4 0.2 copy.47
  76.6 0.1 stack.22
  76.7 15.4 %all_to_all.24 = bf16[4,256,384]{2,1,0:T(8,128)(2,1)S(1)} all-to-all(bf16[4,256,384]{2,1,0:T(8,128)(2,1)S(1)} %stack.22), channel_id=1, replica_groups=mesh['gx'=8,'gy'=8,'gz'=4] {'gz'}, dimensions={0} | all-to-all | bytes 1572864 | tf_op jit(solution)/shard_map/all_to_all | solution.py:22
  92.1 5.5 %fusion = bf16[1024,3072]{0,1:T(8,128)(2,1)} fusion(bf16[384,3072]{1,0:T(8,128)(2,1)S(1)} %copy-done.7, bf16[1024,384]{1,0:T(8,128)(2,1)S(1)} %bitcast.67), kind=kOutput, calls=%fused_computation.7 | convolution fusion | flops 2422210560 | bytes 9437184 | tf_op jit(solution)/shard_map/dot_general | solution.py:126
  97.6 8.6 %copy.58 = bf16[1024,3072]{1,0:T(8,128)(2,1)} copy(bf16[1024,3072]{0,1:T(8,128)(2,1)} %fusion) | data formatting | bytes 12582912
  106.2 0.0 reduce-scatter.12.cloned.1.call-update
  106.3 0.0 reduce-scatter.8.cloned.1.call-start
  106.3 4.6 %pad_maximum_fusion = bf16[64,2,128,128]{3,2,1,0:T(8,128)(2,1)} fusion(bf16[64,1,128,128]{3,2,1,0:T(8,128)(2,1)} %get-tuple-element.49, bf16[64,1,128,128]{3,2,1,0:T(8,128)(2,1)} %get-tuple-element.48), kind=kLoop, calls=%fused_computation.11 | loop fusion | flops 2097152 | bytes 8388608 | tf_op jit(solution)/shard_map/stack | solution.py:88
  110.9 46.8 %all-gather.5.cloned.1.call-done = bf16[1024,3072]{0,1:T(8,128)(2,1)} async-done(((bf16[128,3072]{0,1:T(8,128)(2,1)}), bf16[1024,3072]{0,1:T(8,128)(2,1)}) %all-gather.5.cloned.1.call-update) | async-done | bytes 6291472 | tf_op jit(solution)/shard_map/all_gather | solution.py:87
  157.7 7.0 %multiply_convert_fusion.2 = bf16[384,1024]{1,0:T(8,128)(2,1)} fusion(bf16[384,3072]{1,0:T(8,128)(2,1)} %all-gather.3.cloned.1.call-done, bf16[1024,3072]{0,1:T(8,128)(2,1)} %all-gather.5.cloned.1.call-done), kind=kOutput, calls=%fused_computation.37 | convolution fusion | flops 2416705536 | bytes 9437184 | tf_op jit(solution)/shard_map/dot_general | solution.py:110
  164.7 0.0 reduce-scatter.8.cloned.1.call-update
  164.7 4.7 %copy.48 = bf16[32,2,2,128,128]{4,3,1,2,0:T(8,128)(2,1)} copy(bf16[32,2,2,128,128]{4,3,2,1,0:T(8,128)(2,1)} %bitcast.65) | data formatting | bytes 8388608 | tf_op jit(solution)/shard_map/reshape | solution.py:98
  169.4 7.5 %all-to-all-start.3 = ((bf16[32,2,2,128,128]{4,3,1,2,0:T(8,128)(2,1)}), bf16[32,2,2,128,128]{4,3,1,2,0:T(8,128)(2,1)}, u32[]{:S(2)}, u32[]{:S(2)}) async-start(bf16[32,2,2,128,128]{4,3,1,2,0:T(8,128)(2,1)} %copy.48), calls=%async_computation.4 | async-start | bytes 8388608 | tf_op jit(solution)/shard_map/all_to_all | solution.py:97
  176.8 0.2 reduce-scatter.10.cloned.1.call-start
  177.1 7.7 %fusion.4 = bf16[384,3072]{0,1:T(8,128)(2,1)} fusion(bf16[1024,3072]{0,1:T(8,128)(2,1)} %all-gather.5.cloned.1.call-done, bf16[1024,384]{1,0:T(8,128)(2,1)S(1)} %bitcast.68), kind=kOutput, calls=%fused_computation.18 | convolution fusion | flops 2418278400 | bytes 9437184 | tf_op jit(solution)/shard_map/dot_general | solution.py:116
  184.8 4.3 %copy.56 = bf16[384,3072]{1,0:T(8,128)(2,1)} copy(bf16[384,3072]{0,1:T(8,128)(2,1)} %fusion.4) | data formatting | bytes 4718592
  189.1 0.0 reduce-scatter.10.cloned.1.call-update
  189.2 0.6 copy-done.6
  189.8 0.1 broadcast_bitcast_fusion
  189.8 43.8 %reduce-scatter.12.cloned.1.call-done = bf16[128,3072]{1,0:T(8,128)(2,1)} async-done(((bf16[1024,3072]{1,0:T(8,128)(2,1)}), bf16[128,3072]{1,0:T(8,128)(2,1)}) %reduce-scatter.12.cloned.1.call-update) | async-done | bytes 786448
  233.6 2.3 copy.59
  235.9 0.0 all-to-all-done.3
  235.9 3.2 %copy.49 = f32[32,2,2,128,128]{4,3,1,0,2:T(8,128)S(1)} copy(bf16[32,2,2,128,128]{4,3,1,2,0:T(8,128)(2,1)} %all-to-all-done.3) | data formatting | bytes 12582912 | tf_op jit(solution)/shard_map/reshape | solution.py:105
  239.1 3.8 %slice_bitcast_fusion = (f32[64,128,128]{2,1,0:T(8,128)}, f32[64,128,128]{2,1,0:T(8,128)}) fusion(f32[64,2,128,128]{3,2,0,1:T(8,128)S(1)} %bitcast.64), kind=kLoop, calls=%fused_computation.9 | loop fusion | bytes 16777216 | tf_op jit(solution)/shard_map/squeeze | solution.py:108
  243.0 4.0 %gather_fusion.5 = f32[24,128,128]{2,1,0:T(8,128)} fusion(f32[64,128,128]{2,1,0:T(8,128)} %get-tuple-element.46, s32[1024]{0:T(1024)S(1)} %pad_clamp_fusion), kind=kCustom, calls=%fused_computation.5.clone | custom fusion | bytes 3145824 | tf_op jit(solution)/shard_map/jit(_take)/gather | solution.py:81
  246.9 4.0 %gather_fusion.4 = f32[24,128,128]{2,1,0:T(8,128)} fusion(f32[64,128,128]{2,1,0:T(8,128)} %get-tuple-element.47, s32[1024]{0:T(1024)S(1)} %pad_clamp_fusion), kind=kCustom, calls=%fused_computation.4.clone | custom fusion | bytes 3145824 | tf_op jit(solution)/shard_map/jit(_take)/gather | solution.py:81
  250.9 3.6 %fusion.11 = (f32[1,128,24,128]{3,1,2,0:T(8,128)S(1)}, f32[1,128,24,128]{3,1,2,0:T(8,128)}) fusion(f32[24,128,128]{2,1,0:T(8,128)} %gather_fusion.5, pred[24]{0:T(512)(128)(4,1)S(1)} %compare_and_fusion, f32[24,128,128]{2,1,0:T(8,128)} %gather_fusion.4), kind=kLoop, calls=%fused_computation.32 | loop fusion | flops 1572864 | bytes 6291480 | tf_op jit(solution)/shard_map/mul | solution.py:135
  254.5 3.0 copy.50
  257.6 1.6 copy.51
  259.2 9.5 %multiply_add_fusion = (f32[128,3072]{0,1:T(8,128)}, f32[128,3072]{0,1:T(8,128)}, f32[128,3072]{0,1:T(8,128)S(1)}) fusion(f32[1,128,24,128]{1,3,2,0:T(8,128)S(1)} %copy.46, s32[3072]{0:T(1024)S(1)} %get-tuple-element.55, s32[3072]{0:T(1024)S(1)} %get-tuple-element.56, s32[128]{0:T(128)S(1)} %get-tuple-element.57, s32[128]{0:T(128)S(1)} %get-tuple-element.58, ...), kind=kLoop, calls=%fused_computation.36 | loop fusion | flops 15335424 | bytes 10264704 | tf_op jit(solution)/shard_map/add | solution.py:145
  268.7 3.1 %copy.53 = f32[128,3072]{1,0:T(8,128)} copy(f32[128,3072]{0,1:T(8,128)} %get-tuple-element.43) | data formatting | bytes 3145728
  271.8 1.6 copy.54
  273.5 1.6 copy.55
  275.1 25.1 %reduce-scatter.10.cloned.1.call-done = bf16[48,3072]{1,0:T(8,128)(2,1)} async-done(((bf16[384,3072]{1,0:T(8,128)(2,1)}), bf16[48,3072]{1,0:T(8,128)(2,1)}) %reduce-scatter.10.cloned.1.call-update) | async-done | bytes 294928
  (26 shorter events, 0.1 us)
Async XLA Ops:
  7.2 10.0 %copy-start = (f32[24,128,128]{2,1,0:T(8,128)S(1)}, f32[24,128,128]{2,1,0:T(8,128)}, u32[]{:S(2)}) copy-start(f32[24,128,128]{2,1,0:T(8,128)} %param.12) | copy-start | bytes 4718596
  7.2 60.6 %all-gather.3.cloned.1.call-start = ((), (), s32[]{:S(2)}) async-start(), calls=%async_computation.7 | async-start | bytes 2654208 | tf_op jit(solution)/shard_map/all_gather | solution.py:72
  9.6 23.6 %all-to-all-start.1 = ((s32[32,1,2]{2,1,0:T(1,128)}), s32[32,1,2]{2,1,0:T(1,128)S(1)}, u32[]{:S(2)}, u32[]{:S(2)}) async-start(s32[32,1,2]{2,1,0:T(1,128)} %bitcast.4), calls=%async_computation.1 | async-start | bytes 32768 | tf_op jit(solution)/shard_map/all_to_all | solution.py:66
  17.2 2.8 copy-start.2
  20.0 2.8 copy-start.3
  33.2 34.6 %all-to-all-start = ((bf16[32,2,128,128]{3,2,1,0:T(8,128)(2,1)}), bf16[32,2,128,128]{3,2,1,0:T(8,128)(2,1)}, u32[]{:S(2)}, u32[]{:S(2)}) async-start(bf16[32,2,128,128]{3,2,1,0:T(8,128)(2,1)} %bitcast.66), calls=%async_computation | async-start | bytes 4194304 | tf_op jit(solution)/shard_map/all_to_all | solution.py:69
  40.8 116.8 %all-gather.5.cloned.1.call-start = ((), (), s32[]{:S(2)}) async-start(), calls=%async_computation.8 | async-start | bytes 7077888 | tf_op jit(solution)/shard_map/all_gather | solution.py:87
  75.4 1.0 copy-start.5
  76.4 157.2 %reduce-scatter.12.cloned.1.call-start = ((), (), s32[]{:S(2)}) async-start(), calls=%async_computation.11 | async-start | bytes 7077888
  76.6 15.5 %copy-start.7 = (bf16[384,3072]{1,0:T(8,128)(2,1)S(1)}, bf16[384,3072]{1,0:T(8,128)(2,1)}, u32[]{:S(2)}) copy-start(bf16[384,3072]{1,0:T(8,128)(2,1)} %all-gather.3.cloned.1.call-done) | copy-start | bytes 7077892
  106.3 168.8 %reduce-scatter.8.cloned.1.call-start = ((), (), s32[]{:S(2)}) async-start(), calls=%async_computation.9 | async-start | bytes 983040 | tf_op jit(solution)/shard_map/reduce_scatter | solution.py:111
  169.4 66.5 %all-to-all-start.3 = ((bf16[32,2,2,128,128]{4,3,1,2,0:T(8,128)(2,1)}), bf16[32,2,2,128,128]{4,3,1,2,0:T(8,128)(2,1)}, u32[]{:S(2)}, u32[]{:S(2)}) async-start(bf16[32,2,2,128,128]{4,3,1,2,0:T(8,128)(2,1)} %copy.48), calls=%async_computation.4 | async-start | bytes 8388608 | tf_op jit(solution)/shard_map/all_to_all | solution.py:97
  176.8 123.4 %reduce-scatter.10.cloned.1.call-start = ((), (), s32[]{:S(2)}) async-start(), calls=%async_computation.10 | async-start | bytes 2654208
  189.1 0.7 copy-start.6
  268.7 3.1 %copy-start.4 = (f32[128,3072]{0,1:T(8,128)S(1)}, f32[128,3072]{0,1:T(8,128)}, u32[]{:S(2)}) copy-start(f32[128,3072]{0,1:T(8,128)} %get-tuple-element.44) | copy-start | bytes 4718596
  273.5 26.7 %copy-start.1 = (f32[24,128,128]{2,1,0:T(8,128)S(1)}, f32[24,128,128]{2,1,0:T(8,128)}, u32[]{:S(2)}) copy-start(f32[24,128,128]{2,1,0:T(8,128)} %param.12) | copy-start | bytes 4718596
Sparse Core Ops, SparseCore 0:
  9.8 30.9 all-gather.2
  76.5 81.1 all-gather.4
  160.2 73.3 reduce-scatter.11
  236.6 21.4 reduce-scatter.7
  261.1 39.0 reduce-scatter.9
